TPU v7x, 32 devices: a whole 2x2x4 slice. The times are simulated.
32 devices in a mesh: dp: 4 (over x, core), expert: 8 (over z, y).
Axes of the slice: x: 2, y: 2, z: 4, core: 2. Of those that a mesh axis runs over, the one named last changes fastest.
Arguments:
- latents: bfloat16 [16384, 768], P(('dp', 'expert')), may hold values from -6 to 6
- cotangent: bfloat16 [16384, 768], P(('dp', 'expert')), may hold values from -6 to 6
- expert_of_row: int32 [16384], P(('dp', 'expert')), may hold values from 0 to 7, as said below
- w_in: bfloat16 [8, 768, 1536], P('expert'), may hold values from -0.21875 to 0.21875
- w_out: bfloat16 [8, 1536, 768], P('expert'), may hold values from -0.15625 to 0.15625
Outputs:
- grad_latents: bfloat16 [16384, 768], P(('dp', 'expert'))
- grad_w_in: float32 [8, 768, 1536], P('expert', 'dp')
- grad_w_out: float32 [8, 1536, 768], P('expert', 'dp')
Inputs may be any that keep to these rules, and one draw needn't show every extreme that they name: `expert_of_row`: in every aligned block of 512 rows (the rows of one device) each expert is named by at most 96 rows, and one expert, the same for all blocks, is named by exactly 96 rows in every block.
All inputs are finite; a program needn't handle non-finite values.
Results may differ from a plain program's by a relative error of at most 0.008.
Values may be sent and summed in bfloat16 or wider, within the bound.
No kernel may reach another device: no remote copies, remote signals or barrier semaphores. Data moves between devices by JAX's collectives and lax.ppermute only.
A program may use at most 64 MiB of HBM per device.

v0:
```python
import math

import jax
import jax.numpy as jnp
from jax import lax
from jax.sharding import PartitionSpec as P


def gelu_parts(value):
    coeff = 0.7978845608028654
    cube = value * value * value
    inner = jnp.tanh(coeff * (value + 0.044715 * cube))
    result = 0.5 * value * (1.0 + inner)
    slope = 0.5 * (1.0 + inner) + 0.5 * value * (1.0 - inner * inner) * coeff * (
        1.0 + 3.0 * 0.044715 * value * value
    )
    return (result, slope)


def hidden_pass(block, w_first, w_second):
    width = block.shape[1] // 2
    inputs = block[:, :width]
    grads = block[:, width:]
    pre_act = jnp.dot(inputs, w_first, preferred_element_type=jnp.float32)
    value, slope = gelu_parts(pre_act)
    act = value.astype(jnp.bfloat16)
    act_grad = lax.dot_general(
        grads, w_second, (((1,), (1,)), ((), ())), preferred_element_type=jnp.float32
    )
    hidden_grad = (act_grad * slope).astype(jnp.bfloat16)
    return act, hidden_grad


def row_pass(hidden_grad, w_first):
    return lax.dot_general(
        hidden_grad, w_first, (((1,), (1,)), ((), ())), preferred_element_type=jnp.float32
    ).astype(jnp.bfloat16)


def weight_parts(blocks, acts, hidden_grads):
    width = blocks[0].shape[1] // 2
    block = jnp.concatenate(blocks, axis=0)
    act = jnp.concatenate(acts, axis=0)
    hidden_grad = jnp.concatenate(hidden_grads, axis=0)
    part_in = lax.dot_general(
        block[:, :width], hidden_grad, (((0,), (0,)), ((), ())),
        preferred_element_type=jnp.float32,
    )
    part_out = lax.dot_general(
        act, block[:, width:], (((0,), (0,)), ((), ())), preferred_element_type=jnp.float32
    )
    return part_in, part_out


def halve_dp(blocks, level, groups):
    axis = blocks.ndim - 3
    bit = (lax.axis_index("dp") >> level) & 1
    keep = lax.dynamic_index_in_dim(blocks, bit, axis, keepdims=False)
    send = lax.dynamic_index_in_dim(blocks, 1 - bit, axis, keepdims=False)
    got = lax.ppermute(
        send.astype(jnp.bfloat16), "dp", [(j, j ^ (1 << level)) for j in range(groups)]
    )
    return keep, got


def per_device(latents, cotangent, expert_of_row, w_in, w_out):
    rows, width = latents.shape
    experts = lax.axis_size("expert")
    groups = lax.axis_size("dp")
    capacity = 3 * rows // (2 * experts)
    slots = experts * capacity
    member = (expert_of_row[:, None] == jnp.arange(experts, dtype=jnp.int32)[None, :]).astype(
        jnp.int32
    )
    before = jnp.cumsum(member, axis=0, dtype=jnp.int32) - member
    rank = jnp.sum(before * member, axis=1, dtype=jnp.int32)
    slot = expert_of_row * capacity + rank
    stacked = jnp.concatenate([latents, cotangent], axis=1)
    table = (slot[None, :] == jnp.arange(slots, dtype=jnp.int32)[:, None]).astype(jnp.bfloat16)
    outgoing = jnp.dot(table, stacked, preferred_element_type=jnp.float32).astype(jnp.bfloat16)
    outgoing = outgoing.reshape(experts, capacity, 2 * width)
    w_first = w_in[0]
    w_second = w_out[0]

    first = capacity // 2
    sizes = (first, capacity - first)
    sending = [outgoing[:, :first], outgoing[:, first:]]
    incoming = [lax.all_to_all(sending[0], "expert", 0, 0, tiled=True)]
    sending[1], incoming[0] = lax.optimization_barrier((sending[1], incoming[0]))
    incoming.append(lax.all_to_all(sending[1], "expert", 0, 0, tiled=True))
    scale = 1.0 / math.sqrt(groups * rows)
    levels = groups.bit_length() - 1
    blocks = [incoming[half].reshape(experts * sizes[half], 2 * width) for half in range(2)]
    act, hidden_grad = hidden_pass(blocks[0], w_first, w_second)
    row_grad = row_pass(hidden_grad, w_first)
    incoming_b, row_grad = lax.optimization_barrier((blocks[1], row_grad))
    part_in, part_out = weight_parts([blocks[0]], [act], [hidden_grad])
    back = [lax.all_to_all(row_grad.reshape(experts, sizes[0], width), "expert", 0, 0, tiled=True)]
    inputs_b = incoming_b[:, :width]
    grads_b = incoming_b[:, width:]
    pre_act = jnp.dot(inputs_b, w_first, preferred_element_type=jnp.float32)
    value, slope = gelu_parts(pre_act)
    act = value.astype(jnp.bfloat16)
    part_out = part_out + lax.dot_general(
        act, grads_b, (((0,), (0,)), ((), ())), preferred_element_type=jnp.float32
    )

    def halve_early(part):
        chunked = (scale * part).reshape((2,) * levels + (part.shape[0] // groups,) + part.shape[1:])
        for level in range(levels - 1):
            keep, got = halve_dp(chunked, level, groups)
            chunked = keep + got.astype(jnp.float32)
        return chunked

    sum_out = halve_early(part_out)
    grads_b, slope, sum_out = lax.optimization_barrier((grads_b, slope, sum_out))
    final_out = halve_dp(sum_out, levels - 1, groups)
    act_grad = lax.dot_general(
        grads_b, w_second, (((1,), (1,)), ((), ())), preferred_element_type=jnp.float32
    )
    hidden_grad = (act_grad * slope).astype(jnp.bfloat16)
    part_in = part_in + lax.dot_general(
        inputs_b, hidden_grad, (((0,), (0,)), ((), ())), preferred_element_type=jnp.float32
    )
    sum_in = halve_early(part_in)
    hidden_grad, sum_in = lax.optimization_barrier((hidden_grad, sum_in))
    finals = [final_out, halve_dp(sum_in, levels - 1, groups)]
    row_grad = row_pass(hidden_grad, w_first)
    back[0], row_grad = lax.optimization_barrier((back[0], row_grad))
    back.append(
        lax.all_to_all(row_grad.reshape(experts, sizes[1], width), "expert", 0, 0, tiled=True)
    )
    returned = jnp.concatenate(back, axis=1).reshape(slots, width)
    grad_w_out, grad_w_in = [keep + got.astype(jnp.float32) for keep, got in finals]

    grad_latents = lax.dot_general(
        table, returned, (((0,), (0,)), ((), ())), preferred_element_type=jnp.float32
    )
    grad_latents = grad_latents.astype(jnp.bfloat16)
    return (grad_latents, grad_w_in[None], grad_w_out[None])


def solution(mesh):
    return _sharded(mesh)


def _sharded(mesh):
    return jax.shard_map(
        per_device,
        mesh=mesh,
        in_specs=(
            P(("dp", "expert"), None),
            P(("dp", "expert"), None),
            P(("dp", "expert")),
            P("expert", None, None),
            P("expert", None, None),
        ),
        out_specs=(P(("dp", "expert"), None), P("expert", "dp", None), P("expert", "dp", None)),
        check_vma=False,
    )
```

profile of v0, /device:TPU:0, one launch (start us, length us, event | category | flops | bytes accessed | tf_op | source)
XLA Modules:
  0.0 138.6 jit_solution(12423718249132677440)
XLA Ops:
  4.3 2.8 %convolution_convert_fusion = bf16[768,1536]{1,0:T(8,128)(2,1)S(1)} fusion(bf16[512,768]{1,0:T(8,128)(2,1)} %param.6, bf16[512,768]{1,0:T(8,128)(2,1)} %param.5, s32[512]{0:T(512)S(1)} %multiply_add_fusion), kind=kOutput, calls=%fused_computation.6 | convolution fusion | flops 1212678144 | bytes 3934208 | tf_op jit(solution)/shard_map/dot_general | solution.py:80
  8.3 36.1 %all_to_all.20 = bf16[8,48,1536]{2,1,0:T(8,128)(2,1)} all-to-all(bf16[8,48,1536]{2,1,0:T(8,128)(2,1)S(1)} %get-tuple-element.25), channel_id=1, replica_groups=mesh['dp'=4,'expert'=8] {'expert'}, dimensions={0} | all-to-all | bytes 2359296 | tf_op jit(solution)/shard_map/all_to_all | solution.py:88
  44.4 3.6 %all-to-all-start.1 = ((bf16[8,48,1536]{2,1,0:T(8,128)(2,1)}), bf16[8,48,1536]{2,1,0:T(8,128)(2,1)S(1)}, u32[]{:S(2)}, u32[]{:S(2)}) async-start(bf16[8,48,1536]{2,1,0:T(8,128)(2,1)} %get-tuple-element.14), calls=%async_computation.1 | async-start | bytes 2359296 | tf_op jit(solution)/shard_map/all_to_all | solution.py:90
  48.0 2.3 %fusion.21 = f32[384,1536]{1,0:T(8,128)S(1)} fusion(bf16[1,768,1536]{2,1,0:T(8,128)(2,1)S(1)} %copy-done, bf16[384,1536]{1,0:T(8,128)(2,1)} %bitcast.85), kind=kOutput, calls=%fused_computation.33 | convolution fusion | flops 905969664 | bytes 5308416 | tf_op jit(solution)/shard_map/dot_general | solution.py:24
  50.3 2.0 %fusion = bf16[384,1536]{1,0:T(8,128)(2,1)S(1)} fusion(f32[384,1536]{1,0:T(8,128)S(1)} %fusion.21, bf16[1,1536,768]{2,1,0:T(8,128)(2,1)S(1)} %copy-done.10, bf16[384,1536]{1,0:T(8,128)(2,1)S(1)} %bitcast.87), kind=kOutput, calls=%fused_computation.8 | convolution fusion | flops 917176320 | bytes 6488064 | tf_op jit(solution)/shard_map/dot_general | solution.py:27
  52.3 2.0 %fusion.31 = bf16[384,768]{1,0:T(8,128)(2,1)} fusion(bf16[384,1536]{1,0:T(8,128)(2,1)S(1)} %fusion, bf16[1,768,1536]{2,1,0:T(8,128)(2,1)S(1)} %copy-done), kind=kOutput, calls=%fused_computation.47 | convolution fusion | flops 906264576 | bytes 4128768 | tf_op jit(solution)/shard_map/dot_general | solution.py:35
  54.3 3.7 %fusion.37 = f32[1536,768]{1,0:T(8,128)} fusion(f32[384,1536]{1,0:T(8,128)S(1)} %fusion.21, bf16[384,1536]{1,0:T(8,128)(2,1)S(1)} %bitcast.88), kind=kOutput, calls=%fused_computation.49 | convolution fusion | flops 911278080 | bytes 7667712 | tf_op jit(solution)/shard_map/dot_general | solution.py:49
  58.0 18.1 %all-to-all-done.1 = bf16[8,48,1536]{2,1,0:T(8,128)(2,1)S(1)} async-done(((bf16[8,48,1536]{2,1,0:T(8,128)(2,1)}), bf16[8,48,1536]{2,1,0:T(8,128)(2,1)S(1)}, u32[]{:S(2)}, u32[]{:S(2)}) %all-to-all-start.1) | async-done | bytes 1179680 | tf_op jit(solution)/shard_map/all_to_all | solution.py:90
  76.2 3.5 %fusion.14 = (f32[384,1536]{1,0:T(8,128)}, f32[384,1536]{1,0:T(8,128)S(1)}) fusion(bf16[1,768,1536]{2,1,0:T(8,128)(2,1)S(1)} %copy-done, bf16[384,1536]{1,0:T(8,128)(2,1)S(1)} %bitcast.81), kind=kOutput, calls=%fused_computation.22 | convolution fusion | flops 915996672 | bytes 7667712 | tf_op jit(solution)/shard_map/dot_general | solution.py:101
  81.3 2.1 %copy-done.1 = f32[1536,768]{1,0:T(8,128)} copy-done((f32[1536,768]{1,0:T(8,128)}, f32[1536,768]{1,0:T(8,128)S(1)}, u32[]{:S(2)}) %copy-start.1) | copy-done | bytes 4718616
  84.5 3.0 %fusion.54 = f32[768,1536]{1,0:T(8,128)S(1)} fusion(bf16[384,1536]{1,0:T(8,128)(2,1)} %copy-done.13, bf16[384,1536]{1,0:T(8,128)(2,1)} %bitcast.86), kind=kOutput, calls=%fused_computation.71 | convolution fusion | flops 905969664 | bytes 6488064 | tf_op jit(solution)/shard_map/dot_general | solution.py:45
  87.7 3.2 %bitcast_add_fusion.1 = f32[2,384,768]{2,1,0:T(8,128)} fusion(bf16[2,384,768]{2,1,0:T(8,128)(2,1)} %collective-permute-done, f32[2,2,384,768]{3,2,1,0:T(8,128)S(1)} %bitcast.78, s32[]{:T(128)S(6)} %select_n.20), kind=kLoop, calls=%fused_computation.26 | loop fusion | flops 1179648 | bytes 5898244 | tf_op jit(solution)/shard_map/add | solution.py:112
  93.5 2.1 %copy-done.3 = f32[768,1536]{1,0:T(8,128)} copy-done((f32[768,1536]{1,0:T(8,128)}, f32[768,1536]{1,0:T(8,128)S(1)}, u32[]{:S(2)}) %copy-start.3) | copy-done | bytes 4718616
  97.2 3.7 %all-to-all-start.2 = ((bf16[8,48,768]{2,1,0:T(8,128)(2,1)}), bf16[8,48,768]{2,1,0:T(8,128)(2,1)S(1)}, u32[]{:S(2)}, u32[]{:S(2)}) async-start(bf16[8,48,768]{2,1,0:T(8,128)(2,1)} %bitcast.8), calls=%async_computation.2 | async-start | bytes 1179648 | tf_op jit(solution)/shard_map/all_to_all | solution.py:98
  100.9 2.2 %fusion.53 = bf16[384,768]{1,0:T(8,128)(2,1)} fusion(f32[2,384,768]{2,1,0:T(8,128)} %bitcast_add_fusion.1, s32[]{:T(128)S(6)} %select_n.23), kind=kLoop, calls=%fused_computation.70 | loop fusion | bytes 1179652 | tf_op jit(solution)/shard_map/convert_element_type | solution.py:61
  104.6 2.3 %bitcast_add_fusion = f32[2,192,1536]{2,1,0:T(8,128)S(1)} fusion(bf16[2,192,1536]{2,1,0:T(8,128)(2,1)} %collective-permute-done.1, f32[2,2,192,1536]{3,2,1,0:T(8,128)} %bitcast.80, s32[]{:T(128)S(6)} %select_n.20), kind=kLoop, calls=%fused_computation.25 | loop fusion | flops 1179648 | bytes 5898244 | tf_op jit(solution)/shard_map/add | solution.py:112
  109.8 1.9 %fusion.34 = bf16[384,768]{1,0:T(8,128)(2,1)} fusion(bf16[384,1536]{1,0:T(8,128)(2,1)S(1)} %copy-done.8, bf16[1,768,1536]{2,1,0:T(8,128)(2,1)S(1)} %copy-done), kind=kOutput, calls=%fused_computation.48 | convolution fusion | flops 906264576 | bytes 4128768 | tf_op jit(solution)/shard_map/dot_general | solution.py:35
  111.7 5.3 %all-to-all-done.2 = bf16[8,48,768]{2,1,0:T(8,128)(2,1)S(1)} async-done(((bf16[8,48,768]{2,1,0:T(8,128)(2,1)}), bf16[8,48,768]{2,1,0:T(8,128)(2,1)S(1)}, u32[]{:S(2)}, u32[]{:S(2)}) %all-to-all-start.2) | async-done | bytes 589856 | tf_op jit(solution)/shard_map/all_to_all | solution.py:98
  117.0 3.6 %all-to-all-start.3 = ((bf16[8,48,768]{2,1,0:T(8,128)(2,1)}), bf16[8,48,768]{2,1,0:T(8,128)(2,1)S(1)}, u32[]{:S(2)}, u32[]{:S(2)}) async-start(bf16[8,48,768]{2,1,0:T(8,128)(2,1)} %bitcast.91), calls=%async_computation.3 | async-start | bytes 1179648 | tf_op jit(solution)/shard_map/all_to_all | solution.py:131
  120.7 2.7 %fusion.40 = f32[1,384,768]{2,1,0:T(8,128)} fusion(bf16[384,768]{1,0:T(8,128)(2,1)} %collective-permute-done.3, f32[2,384,768]{2,1,0:T(8,128)} %bitcast_add_fusion.1, s32[]{:T(128)S(6)} %select_n.22), kind=kLoop, calls=%fused_computation.54 | loop fusion | flops 589824 | bytes 2949124 | tf_op jit(solution)/shard_map/broadcast_in_dim | solution.py:140
  123.4 8.0 %collective-permute-done.2 = bf16[192,1536]{1,0:T(8,128)(2,1)} collective-permute-done((bf16[192,1536]{1,0:T(8,128)(2,1)}, bf16[192,1536]{1,0:T(8,128)(2,1)}, u32[]{:S(2)}, u32[]{:S(2)}) %collective-permute-start.2) | collective-permute-done | bytes 589856 | tf_op jit(solution)/shard_map/ppermute | solution.py:60
  131.4 2.2 %fusion.41 = f32[1,192,1536]{2,1,0:T(8,128)} fusion(bf16[192,1536]{1,0:T(8,128)(2,1)} %collective-permute-done.2, f32[2,192,1536]{2,1,0:T(8,128)S(1)} %copy-done.5, s32[]{:T(128)S(6)} %select_n.22), kind=kLoop, calls=%fused_computation.56 | loop fusion | flops 589824 | bytes 2949124 | tf_op jit(solution)/shard_map/broadcast_in_dim | solution.py:140
  133.6 3.2 %all-to-all-done.3 = bf16[8,48,768]{2,1,0:T(8,128)(2,1)S(1)} async-done(((bf16[8,48,768]{2,1,0:T(8,128)(2,1)}), bf16[8,48,768]{2,1,0:T(8,128)(2,1)S(1)}, u32[]{:S(2)}, u32[]{:S(2)}) %all-to-all-start.3) | async-done | bytes 589856 | tf_op jit(solution)/shard_map/all_to_all | solution.py:131
  136.8 1.8 %fusion.30 = bf16[512,768]{1,0:T(8,128)(2,1)} fusion(bf16[768,768]{1,0:T(8,128)(2,1)S(1)} %bitcast.90, s32[512]{0:T(512)S(1)} %multiply_add_fusion), kind=kOutput, calls=%fused_computation.46 | convolution fusion | flops 604766208 | bytes 1968128 | tf_op jit(solution)/shard_map/dot_general | solution.py:136
  (49 shorter events, 16.4 us)
Async XLA Ops:
  0.6 47.3 %copy-start = (bf16[1,768,1536]{2,1,0:T(8,128)(2,1)S(1)}, bf16[1,768,1536]{2,1,0:T(8,128)(2,1)}, u32[]{:S(2)}) copy-start(bf16[1,768,1536]{2,1,0:T(8,128)(2,1)} %param.8) | copy-start | bytes 7077892
  44.4 31.8 %all-to-all-start.1 = ((bf16[8,48,1536]{2,1,0:T(8,128)(2,1)}), bf16[8,48,1536]{2,1,0:T(8,128)(2,1)S(1)}, u32[]{:S(2)}, u32[]{:S(2)}) async-start(bf16[8,48,1536]{2,1,0:T(8,128)(2,1)} %get-tuple-element.14), calls=%async_computation.1 | async-start | bytes 2359296 | tf_op jit(solution)/shard_map/all_to_all | solution.py:90
  48.0 2.3 %copy-start.9 = (bf16[8,48,1536]{2,1,0:T(8,128)(2,1)S(1)}, bf16[8,48,1536]{2,1,0:T(8,128)(2,1)}, u32[]{:S(2)}) copy-start(bf16[8,48,1536]{2,1,0:T(8,128)(2,1)} %all_to_all.20) | copy-start | bytes 3538948
  48.0 2.3 %copy-start.10 = (bf16[1,1536,768]{2,1,0:T(8,128)(2,1)S(1)}, bf16[1,1536,768]{2,1,0:T(8,128)(2,1)}, u32[]{:S(2)}) copy-start(bf16[1,1536,768]{2,1,0:T(8,128)(2,1)} %param.9) | copy-start | bytes 7077892
  52.3 2.0 %copy-start.13 = (bf16[384,1536]{1,0:T(8,128)(2,1)}, bf16[384,1536]{1,0:T(8,128)(2,1)S(1)}, u32[]{:S(2)}) copy-start(bf16[384,1536]{1,0:T(8,128)(2,1)S(1)} %fusion) | copy-start | bytes 3538948
  76.2 3.5 %copy-start.6 = (f32[1536,768]{1,0:T(8,128)S(1)}, f32[1536,768]{1,0:T(8,128)}, u32[]{:S(2)}) copy-start(f32[1536,768]{1,0:T(8,128)} %fusion.37) | copy-start | bytes 14155780
  81.3 2.1 %copy-start.1 = (f32[1536,768]{1,0:T(8,128)}, f32[1536,768]{1,0:T(8,128)S(1)}, u32[]{:S(2)}) copy-start(f32[1536,768]{1,0:T(8,128)S(1)} %add_multiply_fusion.1) | copy-start | bytes 14155780
  84.5 3.2 %collective-permute-start = (bf16[2,384,768]{2,1,0:T(8,128)(2,1)}, bf16[2,384,768]{2,1,0:T(8,128)(2,1)}, u32[]{:S(2)}, u32[]{:S(2)}) collective-permute-start(bf16[2,384,768]{2,1,0:T(8,128)(2,1)} %fusion.38), channel_id=1, source_target_pairs={{0,8},{8,0},{16,24},{24,16},{1,9},{9,1},{17,25},{25,17},{2,10},{10... | collective-permute-start | bytes 3538952 | tf_op jit(solution)/shard_map/ppermute | solution.py:60
  84.5 3.2 %copy-start.2 = (f32[1536,768]{1,0:T(8,128)S(1)}, f32[1536,768]{1,0:T(8,128)}, u32[]{:S(2)}) copy-start(f32[1536,768]{1,0:T(8,128)} %copy-done.1) | copy-start | bytes 14155780
  87.6 3.3 %copy-start.11 = (bf16[1,1536,768]{2,1,0:T(8,128)(2,1)S(1)}, bf16[1,1536,768]{2,1,0:T(8,128)(2,1)}, u32[]{:S(2)}) copy-start(bf16[1,1536,768]{2,1,0:T(8,128)(2,1)} %param.9) | copy-start | bytes 7077892
  87.6 3.3 %copy-start.12 = (f32[384,1536]{1,0:T(8,128)S(1)}, f32[384,1536]{1,0:T(8,128)}, u32[]{:S(2)}) copy-start(f32[384,1536]{1,0:T(8,128)} %get-tuple-element.19) | copy-start | bytes 7077892
  92.0 1.5 %copy-start.7 = (bf16[384,1536]{1,0:T(8,128)(2,1)}, bf16[384,1536]{1,0:T(8,128)(2,1)S(1)}, u32[]{:S(2)}) copy-start(bf16[384,1536]{1,0:T(8,128)(2,1)S(1)} %multiply_convert_fusion) | copy-start | bytes 3538948
  93.5 2.1 %copy-start.3 = (f32[768,1536]{1,0:T(8,128)}, f32[768,1536]{1,0:T(8,128)S(1)}, u32[]{:S(2)}) copy-start(f32[768,1536]{1,0:T(8,128)S(1)} %add_multiply_fusion) | copy-start | bytes 14155780
  96.7 7.9 %collective-permute-start.1 = (bf16[2,192,1536]{2,1,0:T(8,128)(2,1)}, bf16[2,192,1536]{2,1,0:T(8,128)(2,1)}, u32[]{:S(2)}, u32[]{:S(2)}) collective-permute-start(bf16[2,192,1536]{2,1,0:T(8,128)(2,1)} %fusion.39), channel_id=1, source_target_pairs={{0,8},{8,0},{16,24},{24,16},{1,9},{9,1},{17,25},{25,17},{2,10},{10... | collective-permute-start | bytes 3538952 | tf_op jit(solution)/shard_map/ppermute | solution.py:60
  97.2 19.9 %all-to-all-start.2 = ((bf16[8,48,768]{2,1,0:T(8,128)(2,1)}), bf16[8,48,768]{2,1,0:T(8,128)(2,1)S(1)}, u32[]{:S(2)}, u32[]{:S(2)}) async-start(bf16[8,48,768]{2,1,0:T(8,128)(2,1)} %bitcast.8), calls=%async_computation.2 | async-start | bytes 1179648 | tf_op jit(solution)/shard_map/all_to_all | solution.py:98
  103.1 6.7 %copy-start.8 = (bf16[384,1536]{1,0:T(8,128)(2,1)S(1)}, bf16[384,1536]{1,0:T(8,128)(2,1)}, u32[]{:S(2)}) copy-start(bf16[384,1536]{1,0:T(8,128)(2,1)} %copy-done.7) | copy-start | bytes 3538948
  103.1 17.6 %collective-permute-start.3 = (bf16[384,768]{1,0:T(8,128)(2,1)}, bf16[384,768]{1,0:T(8,128)(2,1)}, u32[]{:S(2)}, u32[]{:S(2)}) collective-permute-start(bf16[384,768]{1,0:T(8,128)(2,1)} %fusion.53), channel_id=1, source_target_pairs={{0,16},{8,24},{16,0},{24,8},{1,17},{9,25},{17,1},{25,9},{2,18},{10... | collective-permute-start | bytes 1769480 | tf_op jit(solution)/shard_map/ppermute | solution.py:60
  106.9 1.4 %copy-start.4 = (f32[2,192,1536]{2,1,0:T(8,128)}, f32[2,192,1536]{2,1,0:T(8,128)S(1)}, u32[]{:S(2)}) copy-start(f32[2,192,1536]{2,1,0:T(8,128)S(1)} %bitcast_add_fusion) | copy-start | bytes 7077892
  109.2 22.1 %collective-permute-start.2 = (bf16[192,1536]{1,0:T(8,128)(2,1)}, bf16[192,1536]{1,0:T(8,128)(2,1)}, u32[]{:S(2)}, u32[]{:S(2)}) collective-permute-start(bf16[192,1536]{1,0:T(8,128)(2,1)} %fusion.52), channel_id=1, source_target_pairs={{0,16},{8,24},{16,0},{24,8},{1,17},{9,25},{17,1},{25,9},{2,18},{10... | collective-permute-start | bytes 1769480 | tf_op jit(solution)/shard_map/ppermute | solution.py:60
  117.0 19.7 %all-to-all-start.3 = ((bf16[8,48,768]{2,1,0:T(8,128)(2,1)}), bf16[8,48,768]{2,1,0:T(8,128)(2,1)S(1)}, u32[]{:S(2)}, u32[]{:S(2)}) async-start(bf16[8,48,768]{2,1,0:T(8,128)(2,1)} %bitcast.91), calls=%async_computation.3 | async-start | bytes 1179648 | tf_op jit(solution)/shard_map/all_to_all | solution.py:131
  120.7 10.7 %copy-start.5 = (f32[2,192,1536]{2,1,0:T(8,128)S(1)}, f32[2,192,1536]{2,1,0:T(8,128)}, u32[]{:S(2)}) copy-start(f32[2,192,1536]{2,1,0:T(8,128)} %copy-done.4) | copy-start | bytes 7077892
where the time goes:
time: 139 us
  blocking collectives  36.1 us (26%)
  waiting for transfers between devices  34.7 us (25%)
  matrix products  27.1 us (19%)
  other arithmetic  13.9 us (10%)
  starting transfers between devices  13.4 us (10%)
  local copies, waits for them, and re-layouts  12.5 us (9%)
    all_to_all x1, blocking collectives, per_device(): incoming = [lax.all_to_all(sending[0], 'expert', 0, 0, tiled=True)]  36.1 us
    all_to_all x1, waiting for transfers between devices, per_device(): incoming.append(lax.all_to_all(sending[1], 'expert', 0, 0, tiled=True))  18.1 us
    ppermute x4, waiting for transfers between devices, halve_dp(): lax.ppermute(send.astype(jnp.bfloat16), 'dp', [(j, j ^ 1 << level) for j...  8.08 us
    unnamed x28, local copies, waits for them, and re-layouts  5.71 us
    add x2, other arithmetic, halve_early(): chunked = keep + got.astype(jnp.float32)  5.49 us
    convert_element_type x4, local copies, waits for them, and re-layouts, halve_dp(): send.astype(jnp.bfloat16)  5.35 us
    all_to_all x1, waiting for transfers between devices, per_device(): lax.all_to_all(row_grad.reshape(experts, sizes[0], width), 'expert', 0, 0...  5.33 us
    broadcast_in_dim x2, other arithmetic, per_device(): return (grad_latents, grad_w_in[None], grad_w_out[None])  4.92 us
  transfers between devices with their start and end apart: 7, of which 5 were waited for; matrix products, arithmetic and copies ran while one was open for 18% of the time, Pallas kernels for 0%

commit v1 on v0

--- a/solution.py
+++ b/solution.py
@@ -77,14 +77,23 @@
     slot = expert_of_row * capacity + rank
     stacked = jnp.concatenate([latents, cotangent], axis=1)
     table = (slot[None, :] == jnp.arange(slots, dtype=jnp.int32)[:, None]).astype(jnp.bfloat16)
-    outgoing = jnp.dot(table, stacked, preferred_element_type=jnp.float32).astype(jnp.bfloat16)
-    outgoing = outgoing.reshape(experts, capacity, 2 * width)
     w_first = w_in[0]
     w_second = w_out[0]
 
     first = capacity // 2
     sizes = (first, capacity - first)
-    sending = [outgoing[:, :first], outgoing[:, first:]]
+    sending = []
+    for half in range(2):
+        inside = (rank >= half * first) & (rank < half * first + sizes[half])
+        place = jnp.where(inside, expert_of_row * sizes[half] + rank - half * first, -1)
+        pick = (
+            place[None, :] == jnp.arange(experts * sizes[half], dtype=jnp.int32)[:, None]
+        ).astype(jnp.bfloat16)
+        sending.append(
+            jnp.dot(pick, stacked, preferred_element_type=jnp.float32)
+            .astype(jnp.bfloat16)
+            .reshape(experts, sizes[half], 2 * width)
+        )
     incoming = [lax.all_to_all(sending[0], "expert", 0, 0, tiled=True)]
     sending[1], incoming[0] = lax.optimization_barrier((sending[1], incoming[0]))
     incoming.append(lax.all_to_all(sending[1], "expert", 0, 0, tiled=True))

time: 139 us -> 142 us (1.022)
  blocking collectives: 36.1 us -> 0 us
  waiting for transfers between devices: 34.7 us -> 60.7 us
  starting transfers between devices: 13.4 us -> 20.7 us
  local copies, waits for them, and re-layouts: 12.5 us -> 15.8 us
  matrix products: 27.1 us -> 29.3 us
    all_to_all x1 -> x0, blocking collectives: 36.1 us -> none  [per_device(): incoming = [lax.all_to_all(sending[0], 'expert', 0, 0, tiled=True)]]
    all_to_all x0 -> x1, waiting for transfers between devices: none -> 25.4 us  [per_device(): incoming = [lax.all_to_all(sending[0], 'expert', 0, 0, tiled=True)]]
    all_to_all x0 -> x1, starting transfers between devices: none -> 7.31 us  [per_device(): incoming = [lax.all_to_all(sending[0], 'expert', 0, 0, tiled=True)]]
    unnamed x28 -> x33, local copies, waits for them, and re-layouts: 5.71 us -> 9.07 us
    dot_general x1 -> x2, matrix products: 2.75 us -> 4.98 us  [per_device(): jnp.dot(pick, stacked, preferred_element_type=jnp.float32)]
  transfers between devices with their start and end apart: 7 -> 8, of which waited for: 5 -> 6; matrix products, arithmetic and copies ran while one was open for 18% -> 20% of each run, Pallas kernels for 0% -> 0%
where the time goes in v1:
time: 142 us; the launch traced here: 141 us
  waiting for transfers between devices  60.7 us (43%)
  matrix products  29.3 us (21%)
  starting transfers between devices  20.7 us (15%)
  local copies, waits for them, and re-layouts  15.8 us (11%)
  other arithmetic  13.9 us (10%)
    all_to_all x1, waiting for transfers between devices, per_device(): incoming = [lax.all_to_all(sending[0], 'expert', 0, 0, tiled=True)]  25.4 us
    all_to_all x1, waiting for transfers between devices, per_device(): incoming.append(lax.all_to_all(sending[1], 'expert', 0, 0, tiled=True))  18.7 us
    unnamed x33, local copies, waits for them, and re-layouts  9.07 us
    ppermute x4, waiting for transfers between devices, halve_dp(): lax.ppermute(send.astype(jnp.bfloat16), 'dp', [(j, j ^ 1 << level) for j...  8.04 us
    all_to_all x1, starting transfers between devices, per_device(): incoming = [lax.all_to_all(sending[0], 'expert', 0, 0, tiled=True)]  7.31 us
    add x2, other arithmetic, halve_early(): chunked = keep + got.astype(jnp.float32)  5.49 us
    all_to_all x1, waiting for transfers between devices, per_device(): lax.all_to_all(row_grad.reshape(experts, sizes[0], width), 'expert', 0, 0...  5.38 us
    convert_element_type x4, local copies, waits for them, and re-layouts, halve_dp(): send.astype(jnp.bfloat16)  5.31 us
  transfers between devices with their start and end apart: 8, of which 6 were waited for; matrix products, arithmetic and copies ran while one was open for 20% of the time, Pallas kernels for 0%

profile of v1, /device:TPU:0, one launch (start us, length us, event | category | flops | bytes accessed | tf_op | source)
XLA Modules:
  0.0 141.4 jit_solution(14997663554065120898)
XLA Ops:
  9.7 7.3 %all-to-all-start = ((bf16[8,48,1536]{2,1,0:T(8,128)(2,1)}), bf16[8,48,1536]{2,1,0:T(8,128)(2,1)S(1)}, u32[]{:S(2)}, u32[]{:S(2)}) async-start(bf16[8,48,1536]{2,1,0:T(8,128)(2,1)} %bitcast.93), calls=%async_computation | async-start | bytes 2359296 | tf_op jit(solution)/shard_map/all_to_all | solution.py:97
  17.0 3.2 %convolution_convert_fusion.1 = bf16[384,1536]{1,0:T(8,128)(2,1)} fusion(bf16[512,1536]{1,0:T(8,128)(2,1)} %copy-done.15, s32[512]{0:T(512)S(1)} %get-tuple-element.26), kind=kOutput, calls=%fused_computation.9 | convolution fusion | flops 604766208 | bytes 2754560 | tf_op jit(solution)/shard_map/dot_general | solution.py:93
  20.2 25.4 %all-to-all-done = bf16[8,48,1536]{2,1,0:T(8,128)(2,1)S(1)} async-done(((bf16[8,48,1536]{2,1,0:T(8,128)(2,1)}), bf16[8,48,1536]{2,1,0:T(8,128)(2,1)S(1)}, u32[]{:S(2)}, u32[]{:S(2)}) %all-to-all-start) | async-done | bytes 1179680 | tf_op jit(solution)/shard_map/all_to_all | solution.py:97
  46.6 3.6 %all-to-all-start.1 = ((bf16[8,48,1536]{2,1,0:T(8,128)(2,1)}), bf16[8,48,1536]{2,1,0:T(8,128)(2,1)S(1)}, u32[]{:S(2)}, u32[]{:S(2)}) async-start(bf16[8,48,1536]{2,1,0:T(8,128)(2,1)} %bitcast.92), calls=%async_computation.1 | async-start | bytes 2359296 | tf_op jit(solution)/shard_map/all_to_all | solution.py:99
  50.2 2.3 %fusion.21 = f32[384,1536]{1,0:T(8,128)S(1)} fusion(bf16[1,768,1536]{2,1,0:T(8,128)(2,1)S(1)} %copy-done, bf16[384,1536]{1,0:T(8,128)(2,1)} %bitcast.88), kind=kOutput, calls=%fused_computation.34 | convolution fusion | flops 905969664 | bytes 5308416 | tf_op jit(solution)/shard_map/dot_general | solution.py:24
  52.6 2.0 %fusion = bf16[384,1536]{1,0:T(8,128)(2,1)S(1)} fusion(f32[384,1536]{1,0:T(8,128)S(1)} %fusion.21, bf16[1,1536,768]{2,1,0:T(8,128)(2,1)S(1)} %copy-done.11, bf16[384,1536]{1,0:T(8,128)(2,1)S(1)} %bitcast.90), kind=kOutput, calls=%fused_computation.7 | convolution fusion | flops 917176320 | bytes 6488064 | tf_op jit(solution)/shard_map/dot_general | solution.py:27
  54.6 2.0 %fusion.28 = bf16[384,768]{1,0:T(8,128)(2,1)} fusion(bf16[384,1536]{1,0:T(8,128)(2,1)S(1)} %fusion, bf16[1,768,1536]{2,1,0:T(8,128)(2,1)S(1)} %copy-done), kind=kOutput, calls=%fused_computation.45 | convolution fusion | flops 906264576 | bytes 4128768 | tf_op jit(solution)/shard_map/dot_general | solution.py:35
  56.5 3.7 %fusion.34 = f32[1536,768]{1,0:T(8,128)} fusion(f32[384,1536]{1,0:T(8,128)S(1)} %fusion.21, bf16[384,1536]{1,0:T(8,128)(2,1)S(1)} %bitcast.91), kind=kOutput, calls=%fused_computation.47 | convolution fusion | flops 911278080 | bytes 7667712 | tf_op jit(solution)/shard_map/dot_general | solution.py:49
  60.3 18.7 %all-to-all-done.1 = bf16[8,48,1536]{2,1,0:T(8,128)(2,1)S(1)} async-done(((bf16[8,48,1536]{2,1,0:T(8,128)(2,1)}), bf16[8,48,1536]{2,1,0:T(8,128)(2,1)S(1)}, u32[]{:S(2)}, u32[]{:S(2)}) %all-to-all-start.1) | async-done | bytes 1179680 | tf_op jit(solution)/shard_map/all_to_all | solution.py:99
  79.0 3.5 %fusion.14 = (f32[384,1536]{1,0:T(8,128)}, f32[384,1536]{1,0:T(8,128)S(1)}) fusion(bf16[1,768,1536]{2,1,0:T(8,128)(2,1)S(1)} %copy-done, bf16[384,1536]{1,0:T(8,128)(2,1)S(1)} %bitcast.84), kind=kOutput, calls=%fused_computation.23 | convolution fusion | flops 915996672 | bytes 7667712 | tf_op jit(solution)/shard_map/dot_general | solution.py:110
  84.1 2.1 %copy-done.1 = f32[1536,768]{1,0:T(8,128)} copy-done((f32[1536,768]{1,0:T(8,128)}, f32[1536,768]{1,0:T(8,128)S(1)}, u32[]{:S(2)}) %copy-start.1) | copy-done | bytes 4718616
  87.3 3.0 %fusion.50 = f32[768,1536]{1,0:T(8,128)S(1)} fusion(bf16[384,1536]{1,0:T(8,128)(2,1)} %copy-done.14, bf16[384,1536]{1,0:T(8,128)(2,1)} %bitcast.89), kind=kOutput, calls=%fused_computation.70 | convolution fusion | flops 905969664 | bytes 6488064 | tf_op jit(solution)/shard_map/dot_general | solution.py:45
  90.5 3.2 %bitcast_add_fusion.1 = f32[2,384,768]{2,1,0:T(8,128)} fusion(bf16[2,384,768]{2,1,0:T(8,128)(2,1)} %collective-permute-done, f32[2,2,384,768]{3,2,1,0:T(8,128)S(1)} %bitcast.81, s32[]{:T(128)S(6)} %select_n.29), kind=kLoop, calls=%fused_computation.27 | loop fusion | flops 1179648 | bytes 5898244 | tf_op jit(solution)/shard_map/add | solution.py:121
  96.3 2.1 %copy-done.3 = f32[768,1536]{1,0:T(8,128)} copy-done((f32[768,1536]{1,0:T(8,128)}, f32[768,1536]{1,0:T(8,128)S(1)}, u32[]{:S(2)}) %copy-start.3) | copy-done | bytes 4718616
  100.0 3.7 %all-to-all-start.2 = ((bf16[8,48,768]{2,1,0:T(8,128)(2,1)}), bf16[8,48,768]{2,1,0:T(8,128)(2,1)S(1)}, u32[]{:S(2)}, u32[]{:S(2)}) async-start(bf16[8,48,768]{2,1,0:T(8,128)(2,1)} %bitcast.9), calls=%async_computation.2 | async-start | bytes 1179648 | tf_op jit(solution)/shard_map/all_to_all | solution.py:107
  103.7 2.2 %fusion.49 = bf16[384,768]{1,0:T(8,128)(2,1)} fusion(f32[2,384,768]{2,1,0:T(8,128)} %bitcast_add_fusion.1, s32[]{:T(128)S(6)} %select_n.32), kind=kLoop, calls=%fused_computation.69 | loop fusion | bytes 1179652 | tf_op jit(solution)/shard_map/convert_element_type | solution.py:61
  107.4 2.3 %bitcast_add_fusion = f32[2,192,1536]{2,1,0:T(8,128)S(1)} fusion(bf16[2,192,1536]{2,1,0:T(8,128)(2,1)} %collective-permute-done.1, f32[2,2,192,1536]{3,2,1,0:T(8,128)} %bitcast.83, s32[]{:T(128)S(6)} %select_n.29), kind=kLoop, calls=%fused_computation.26 | loop fusion | flops 1179648 | bytes 5898244 | tf_op jit(solution)/shard_map/add | solution.py:121
  112.5 1.9 %fusion.31 = bf16[384,768]{1,0:T(8,128)(2,1)} fusion(bf16[384,1536]{1,0:T(8,128)(2,1)S(1)} %copy-done.8, bf16[1,768,1536]{2,1,0:T(8,128)(2,1)S(1)} %copy-done), kind=kOutput, calls=%fused_computation.46 | convolution fusion | flops 906264576 | bytes 4128768 | tf_op jit(solution)/shard_map/dot_general | solution.py:35
  114.5 5.4 %all-to-all-done.2 = bf16[8,48,768]{2,1,0:T(8,128)(2,1)S(1)} async-done(((bf16[8,48,768]{2,1,0:T(8,128)(2,1)}), bf16[8,48,768]{2,1,0:T(8,128)(2,1)S(1)}, u32[]{:S(2)}, u32[]{:S(2)}) %all-to-all-start.2) | async-done | bytes 589856 | tf_op jit(solution)/shard_map/all_to_all | solution.py:107
  119.8 3.6 %all-to-all-start.3 = ((bf16[8,48,768]{2,1,0:T(8,128)(2,1)}), bf16[8,48,768]{2,1,0:T(8,128)(2,1)S(1)}, u32[]{:S(2)}, u32[]{:S(2)}) async-start(bf16[8,48,768]{2,1,0:T(8,128)(2,1)} %bitcast.95), calls=%async_computation.3 | async-start | bytes 1179648 | tf_op jit(solution)/shard_map/all_to_all | solution.py:140
  123.5 2.7 %fusion.37 = f32[1,384,768]{2,1,0:T(8,128)} fusion(bf16[384,768]{1,0:T(8,128)(2,1)} %collective-permute-done.3, f32[2,384,768]{2,1,0:T(8,128)} %bitcast_add_fusion.1, s32[]{:T(128)S(6)} %select_n.31), kind=kLoop, calls=%fused_computation.52 | loop fusion | flops 589824 | bytes 2949124 | tf_op jit(solution)/shard_map/broadcast_in_dim | solution.py:149
  126.2 7.9 %collective-permute-done.2 = bf16[192,1536]{1,0:T(8,128)(2,1)} collective-permute-done((bf16[192,1536]{1,0:T(8,128)(2,1)}, bf16[192,1536]{1,0:T(8,128)(2,1)}, u32[]{:S(2)}, u32[]{:S(2)}) %collective-permute-start.2) | collective-permute-done | bytes 589856 | tf_op jit(solution)/shard_map/ppermute | solution.py:60
  134.1 2.2 %fusion.38 = f32[1,192,1536]{2,1,0:T(8,128)} fusion(bf16[192,1536]{1,0:T(8,128)(2,1)} %collective-permute-done.2, f32[2,192,1536]{2,1,0:T(8,128)S(1)} %copy-done.5, s32[]{:T(128)S(6)} %select_n.31), kind=kLoop, calls=%fused_computation.54 | loop fusion | flops 589824 | bytes 2949124 | tf_op jit(solution)/shard_map/broadcast_in_dim | solution.py:149
  136.3 3.2 %all-to-all-done.3 = bf16[8,48,768]{2,1,0:T(8,128)(2,1)S(1)} async-done(((bf16[8,48,768]{2,1,0:T(8,128)(2,1)}), bf16[8,48,768]{2,1,0:T(8,128)(2,1)S(1)}, u32[]{:S(2)}, u32[]{:S(2)}) %all-to-all-start.3) | async-done | bytes 589856 | tf_op jit(solution)/shard_map/all_to_all | solution.py:140
  (56 shorter events, 23.3 us)
Async XLA Ops:
  0.6 49.6 %copy-start = (bf16[1,768,1536]{2,1,0:T(8,128)(2,1)S(1)}, bf16[1,768,1536]{2,1,0:T(8,128)(2,1)}, u32[]{:S(2)}) copy-start(bf16[1,768,1536]{2,1,0:T(8,128)(2,1)} %param.8) | copy-start | bytes 7077892
  6.7 1.2 copy-start.15
  9.7 35.9 %all-to-all-start = ((bf16[8,48,1536]{2,1,0:T(8,128)(2,1)}), bf16[8,48,1536]{2,1,0:T(8,128)(2,1)S(1)}, u32[]{:S(2)}, u32[]{:S(2)}) async-start(bf16[8,48,1536]{2,1,0:T(8,128)(2,1)} %bitcast.93), calls=%async_computation | async-start | bytes 2359296 | tf_op jit(solution)/shard_map/all_to_all | solution.py:97
  45.6 1.0 copy-start.9
  46.6 32.4 %all-to-all-start.1 = ((bf16[8,48,1536]{2,1,0:T(8,128)(2,1)}), bf16[8,48,1536]{2,1,0:T(8,128)(2,1)S(1)}, u32[]{:S(2)}, u32[]{:S(2)}) async-start(bf16[8,48,1536]{2,1,0:T(8,128)(2,1)} %bitcast.92), calls=%async_computation.1 | async-start | bytes 2359296 | tf_op jit(solution)/shard_map/all_to_all | solution.py:99
  50.2 2.3 %copy-start.10 = (bf16[8,48,1536]{2,1,0:T(8,128)(2,1)S(1)}, bf16[8,48,1536]{2,1,0:T(8,128)(2,1)}, u32[]{:S(2)}) copy-start(bf16[8,48,1536]{2,1,0:T(8,128)(2,1)} %copy-done.9) | copy-start | bytes 3538948
  50.2 2.3 %copy-start.11 = (bf16[1,1536,768]{2,1,0:T(8,128)(2,1)S(1)}, bf16[1,1536,768]{2,1,0:T(8,128)(2,1)}, u32[]{:S(2)}) copy-start(bf16[1,1536,768]{2,1,0:T(8,128)(2,1)} %param.9) | copy-start | bytes 7077892
  54.6 2.0 %copy-start.14 = (bf16[384,1536]{1,0:T(8,128)(2,1)}, bf16[384,1536]{1,0:T(8,128)(2,1)S(1)}, u32[]{:S(2)}) copy-start(bf16[384,1536]{1,0:T(8,128)(2,1)S(1)} %fusion) | copy-start | bytes 3538948
  79.0 3.5 %copy-start.6 = (f32[1536,768]{1,0:T(8,128)S(1)}, f32[1536,768]{1,0:T(8,128)}, u32[]{:S(2)}) copy-start(f32[1536,768]{1,0:T(8,128)} %fusion.34) | copy-start | bytes 14155780
  84.1 2.1 %copy-start.1 = (f32[1536,768]{1,0:T(8,128)}, f32[1536,768]{1,0:T(8,128)S(1)}, u32[]{:S(2)}) copy-start(f32[1536,768]{1,0:T(8,128)S(1)} %add_multiply_fusion.1) | copy-start | bytes 14155780
  87.3 3.2 %collective-permute-start = (bf16[2,384,768]{2,1,0:T(8,128)(2,1)}, bf16[2,384,768]{2,1,0:T(8,128)(2,1)}, u32[]{:S(2)}, u32[]{:S(2)}) collective-permute-start(bf16[2,384,768]{2,1,0:T(8,128)(2,1)} %fusion.35), channel_id=1, source_target_pairs={{0,8},{8,0},{16,24},{24,16},{1,9},{9,1},{17,25},{25,17},{2,10},{10... | collective-permute-start | bytes 3538952 | tf_op jit(solution)/shard_map/ppermute | solution.py:60
  87.3 3.2 %copy-start.2 = (f32[1536,768]{1,0:T(8,128)S(1)}, f32[1536,768]{1,0:T(8,128)}, u32[]{:S(2)}) copy-start(f32[1536,768]{1,0:T(8,128)} %copy-done.1) | copy-start | bytes 14155780
  90.4 3.3 %copy-start.12 = (bf16[1,1536,768]{2,1,0:T(8,128)(2,1)S(1)}, bf16[1,1536,768]{2,1,0:T(8,128)(2,1)}, u32[]{:S(2)}) copy-start(bf16[1,1536,768]{2,1,0:T(8,128)(2,1)} %param.9) | copy-start | bytes 7077892
  90.4 3.3 %copy-start.13 = (f32[384,1536]{1,0:T(8,128)S(1)}, f32[384,1536]{1,0:T(8,128)}, u32[]{:S(2)}) copy-start(f32[384,1536]{1,0:T(8,128)} %get-tuple-element.19) | copy-start | bytes 7077892
  94.8 1.5 %copy-start.7 = (bf16[384,1536]{1,0:T(8,128)(2,1)}, bf16[384,1536]{1,0:T(8,128)(2,1)S(1)}, u32[]{:S(2)}) copy-start(bf16[384,1536]{1,0:T(8,128)(2,1)S(1)} %multiply_convert_fusion) | copy-start | bytes 3538948
  96.3 2.1 %copy-start.3 = (f32[768,1536]{1,0:T(8,128)}, f32[768,1536]{1,0:T(8,128)S(1)}, u32[]{:S(2)}) copy-start(f32[768,1536]{1,0:T(8,128)S(1)} %add_multiply_fusion) | copy-start | bytes 14155780
  99.5 7.8 %collective-permute-start.1 = (bf16[2,192,1536]{2,1,0:T(8,128)(2,1)}, bf16[2,192,1536]{2,1,0:T(8,128)(2,1)}, u32[]{:S(2)}, u32[]{:S(2)}) collective-permute-start(bf16[2,192,1536]{2,1,0:T(8,128)(2,1)} %fusion.36), channel_id=1, source_target_pairs={{0,8},{8,0},{16,24},{24,16},{1,9},{9,1},{17,25},{25,17},{2,10},{10... | collective-permute-start | bytes 3538952 | tf_op jit(solution)/shard_map/ppermute | solution.py:60
  100.0 19.9 %all-to-all-start.2 = ((bf16[8,48,768]{2,1,0:T(8,128)(2,1)}), bf16[8,48,768]{2,1,0:T(8,128)(2,1)S(1)}, u32[]{:S(2)}, u32[]{:S(2)}) async-start(bf16[8,48,768]{2,1,0:T(8,128)(2,1)} %bitcast.9), calls=%async_computation.2 | async-start | bytes 1179648 | tf_op jit(solution)/shard_map/all_to_all | solution.py:107
  105.9 6.7 %copy-start.8 = (bf16[384,1536]{1,0:T(8,128)(2,1)S(1)}, bf16[384,1536]{1,0:T(8,128)(2,1)}, u32[]{:S(2)}) copy-start(bf16[384,1536]{1,0:T(8,128)(2,1)} %copy-done.7) | copy-start | bytes 3538948
  105.9 17.6 %collective-permute-start.3 = (bf16[384,768]{1,0:T(8,128)(2,1)}, bf16[384,768]{1,0:T(8,128)(2,1)}, u32[]{:S(2)}, u32[]{:S(2)}) collective-permute-start(bf16[384,768]{1,0:T(8,128)(2,1)} %fusion.49), channel_id=1, source_target_pairs={{0,16},{8,24},{16,0},{24,8},{1,17},{9,25},{17,1},{25,9},{2,18},{10... | collective-permute-start | bytes 1769480 | tf_op jit(solution)/shard_map/ppermute | solution.py:60
  109.7 1.4 %copy-start.4 = (f32[2,192,1536]{2,1,0:T(8,128)}, f32[2,192,1536]{2,1,0:T(8,128)S(1)}, u32[]{:S(2)}) copy-start(f32[2,192,1536]{2,1,0:T(8,128)S(1)} %bitcast_add_fusion) | copy-start | bytes 7077892
  112.0 22.1 %collective-permute-start.2 = (bf16[192,1536]{1,0:T(8,128)(2,1)}, bf16[192,1536]{1,0:T(8,128)(2,1)}, u32[]{:S(2)}, u32[]{:S(2)}) collective-permute-start(bf16[192,1536]{1,0:T(8,128)(2,1)} %fusion.48), channel_id=1, source_target_pairs={{0,16},{8,24},{16,0},{24,8},{1,17},{9,25},{17,1},{25,9},{2,18},{10... | collective-permute-start | bytes 1769480 | tf_op jit(solution)/shard_map/ppermute | solution.py:60
  119.8 19.7 %all-to-all-start.3 = ((bf16[8,48,768]{2,1,0:T(8,128)(2,1)}), bf16[8,48,768]{2,1,0:T(8,128)(2,1)S(1)}, u32[]{:S(2)}, u32[]{:S(2)}) async-start(bf16[8,48,768]{2,1,0:T(8,128)(2,1)} %bitcast.95), calls=%async_computation.3 | async-start | bytes 1179648 | tf_op jit(solution)/shard_map/all_to_all | solution.py:140
  123.5 10.7 %copy-start.5 = (f32[2,192,1536]{2,1,0:T(8,128)S(1)}, f32[2,192,1536]{2,1,0:T(8,128)}, u32[]{:S(2)}) copy-start(f32[2,192,1536]{2,1,0:T(8,128)} %copy-done.4) | copy-start | bytes 7077892
